TPU v7x, 128 devices: a whole 4x4x4 slice. The times are simulated.
128 devices in a mesh: req: 4 (over z), seq: 32 (over x, y, core).
Axes of the slice: x: 4, y: 4, z: 4, core: 2. Of those that a mesh axis runs over, the one named last changes fastest.
Arguments:
- short_tokens: bfloat16 [256, 4, 1024], P(('req', 'seq')), may hold values from -6 to 6
- long_tokens: bfloat16 [8, 4, 1024], P('req'), may hold values from -6 to 6
- short_keys: bfloat16 [256, 1024, 1024], P(('req', 'seq'))
- short_values: bfloat16 [256, 1024, 1024], P(('req', 'seq')), may hold values from -6 to 6
- long_keys: bfloat16 [8, 8192, 1024], P('req', 'seq')
- long_values: bfloat16 [8, 8192, 1024], P('req', 'seq'), may hold values from -6 to 6
- short_lengths: int32 [256], P(('req', 'seq')), may hold values from 512 to 1024
- long_lengths: int32 [8], P('req'), may hold values from 4096 to 8192
- attn_gain: float32 [1024], replicated, may hold values from 0.5 to 1.5
- ffn_gain: float32 [1024], replicated, may hold values from 0.5 to 1.5
- w_query: bfloat16 [1024, 1024], P(None, 'req'), may hold values from -0.1875 to 0.1875
- w_key: bfloat16 [1024, 1024], P(None, 'req'), may hold values from -0.1875 to 0.1875
- w_value: bfloat16 [1024, 1024], P(None, 'req'), may hold values from -0.1875 to 0.1875
- w_out: bfloat16 [1024, 1024], P('req'), may hold values from -0.1875 to 0.1875
- w_up: bfloat16 [1024, 4096], P(None, 'req'), may hold values from -0.1875 to 0.1875
- w_down: bfloat16 [4096, 1024], P('req'), may hold values from -0.09375 to 0.09375
Outputs:
- short_hidden: bfloat16 [256, 4, 1024], P(('req', 'seq'))
- long_hidden: bfloat16 [8, 4, 1024], P('req')
- short_new_keys: bfloat16 [256, 4, 1024], P(('req', 'seq'))
- short_new_values: bfloat16 [256, 4, 1024], P(('req', 'seq'))
- long_new_keys: bfloat16 [8, 4, 1024], P('req')
- long_new_values: bfloat16 [8, 4, 1024], P('req')
All inputs are finite; a program needn't handle non-finite values.
Results may differ from a plain program's by a relative error of at most 0.011.
Values may be sent and summed in bfloat16 or wider, within the bound.
No kernel may reach another device: no remote copies, remote signals or barrier semaphores. Data moves between devices by JAX's collectives and lax.ppermute only.
A program may use at most 128 MiB of HBM per device.

v0:
```python
import jax
import jax.numpy as jnp
from jax import lax
from jax.sharding import PartitionSpec as P

H = 16
HD = 64
masked_score = -1e30


def layer_norm(rows, gain):
    mean = jnp.mean(rows, axis=-1, keepdims=True)
    centred = rows - mean
    spread = jnp.mean(centred * centred, axis=-1, keepdims=True)
    return centred * lax.rsqrt(spread + 1e-05) * gain


def partial_block(query, keys, values, valid):
    scores = jnp.einsum("rthd,rphd->rhtp", query, keys, preferred_element_type=jnp.float32) * 0.125
    scores = jnp.where(valid, scores, masked_score)
    peak = jnp.max(scores, axis=-1)
    weights = jnp.where(valid, jnp.exp(scores - peak[..., None]), 0.0)
    total = jnp.sum(weights, axis=-1)
    output = jnp.einsum(
        "rhtp,rphd->rhtd", weights.astype(jnp.bfloat16), values, preferred_element_type=jnp.float32
    )
    return (peak, total, output)


def join(first, second):
    peak = jnp.maximum(first[0], second[0])
    scale_one = jnp.exp(first[0] - peak)
    scale_two = jnp.exp(second[0] - peak)
    total = first[1] * scale_one + second[1] * scale_two
    output = first[2] * scale_one[..., None] + second[2] * scale_two[..., None]
    return (peak, total, output)


def merge_long(partial_value):
    peak, total, output = partial_value
    top = lax.pmax(peak, "seq")
    scale = jnp.exp(peak - top)
    total_sum, output_sum = lax.psum((total * scale, output * scale[..., None]), "seq")
    return (top, total_sum, output_sum)


def shards(
    short_tokens,
    long_tokens,
    short_keys,
    short_values,
    long_keys,
    long_values,
    short_lengths,
    long_lengths,
    attn_gain,
    ffn_gain,
    w_query,
    w_key,
    w_value,
    w_out,
    w_up,
    w_down,
):
    short_count = short_tokens.shape[0]
    long_count = long_tokens.shape[0]
    steps = short_tokens.shape[1]
    width = short_tokens.shape[2]
    req_count = short_count + long_count
    rows_count = req_count * steps
    groups = lax.axis_size("req")
    block = long_keys.shape[1]
    anchor = lax.axis_index("seq") * block
    cache_short_k = short_keys.reshape(short_count, short_keys.shape[1], H, HD)
    cache_short_v = short_values.reshape(short_count, short_keys.shape[1], H, HD)
    cache_long_k = long_keys.reshape(long_count, block, H, HD)
    cache_long_v = long_values.reshape(long_count, block, H, HD)
    short_valid = (jnp.arange(short_keys.shape[1])[None, :] < short_lengths[:, None])[
        :, None, None, :
    ]
    long_valid = ((anchor + jnp.arange(block))[None, :] < long_lengths[:, None])[:, None, None, :]
    stacked = jnp.concatenate([w_query, w_key, w_value], 1)
    local = w_query.shape[1]
    fresh_ids = jnp.arange(steps)
    fresh_valid = (fresh_ids[None, :] <= fresh_ids[:, None])[None, None, :, :]
    rows = (
        jnp.concatenate([short_tokens, long_tokens], 0)
        .reshape(rows_count, width)
        .astype(jnp.float32)
    )
    normed = layer_norm(rows, attn_gain).astype(jnp.bfloat16)
    project_spread = jnp.dot(
        lax.all_gather(normed, "req", axis=0, tiled=True),
        stacked,
        preferred_element_type=jnp.float32,
    ).astype(jnp.bfloat16)
    moved = lax.all_to_all(project_spread, "req", split_axis=0, concat_axis=1, tiled=True)
    moved = moved.reshape(rows_count, groups, 3, local)
    query = moved[:, :, 0].reshape(req_count, steps, H, HD)
    key_now = moved[:, :, 1].reshape(req_count, steps, width)
    value_now = moved[:, :, 2].reshape(req_count, steps, width)
    fresh_k = key_now.reshape(req_count, steps, H, HD)
    fresh_v = value_now.reshape(req_count, steps, H, HD)
    fresh = partial_block(query, fresh_k, fresh_v, fresh_valid)
    short_part = partial_block(query[:short_count], cache_short_k, cache_short_v, short_valid)
    long_part = merge_long(
        partial_block(query[short_count:], cache_long_k, cache_long_v, long_valid)
    )
    cache_part = jax.tree.map(
        lambda first, second: jnp.concatenate([first, second], 0), short_part, long_part
    )
    peak, total, output = join(cache_part, fresh)
    attended = output / total[..., None]
    attended = attended.transpose(0, 2, 1, 3).reshape(rows_count, width).astype(jnp.bfloat16)
    spread = lax.all_to_all(attended, "req", split_axis=1, concat_axis=0, tiled=True)
    mixed = rows + lax.psum_scatter(
        jnp.dot(spread, w_out, preferred_element_type=jnp.float32),
        "req",
        scatter_dimension=0,
        tiled=True,
    )
    normed_ffn = layer_norm(mixed, ffn_gain).astype(jnp.bfloat16)
    hidden = jax.nn.gelu(
        jnp.dot(
            lax.all_gather(normed_ffn, "req", axis=0, tiled=True),
            w_up,
            preferred_element_type=jnp.float32,
        ),
        approximate=False,
    ).astype(jnp.bfloat16)
    result = mixed + lax.psum_scatter(
        jnp.dot(hidden, w_down, preferred_element_type=jnp.float32),
        "req",
        scatter_dimension=0,
        tiled=True,
    )
    states = result.astype(jnp.bfloat16).reshape(req_count, steps, width)
    return (
        states[:short_count],
        states[short_count:],
        key_now[:short_count],
        value_now[:short_count],
        key_now[short_count:],
        value_now[short_count:],
    )


def solution(mesh):
    in_specs = (
        P(("req", "seq"), None, None),
        P("req", None, None),
        P(("req", "seq"), None, None),
        P(("req", "seq"), None, None),
        P("req", "seq", None),
        P("req", "seq", None),
        P(("req", "seq")),
        P("req"),
        P(),
        P(),
        P(None, "req"),
        P(None, "req"),
        P(None, "req"),
        P("req", None),
        P(None, "req"),
        P("req", None),
    )
    out_specs = (
        P(("req", "seq"), None, None),
        P("req", None, None),
        P(("req", "seq"), None, None),
        P(("req", "seq"), None, None),
        P("req", None, None),
        P("req", None, None),
    )
    return jax.shard_map(shards, mesh=mesh, in_specs=in_specs, out_specs=out_specs, check_vma=False)
```

profile of v0, /device:TPU:0, one launch (start us, length us, event | category | flops | bytes accessed | tf_op | source)
XLA Modules:
  0.0 382.5 jit_solution(11535167643442120678)
XLA Ops:
  7.2 1.0 fusion.115
  8.3 0.9 multiply_reduce_fusion.1
  9.2 0.8 maximum_convert_fusion
  10.1 0.8 multiply_convert_fusion.1
  10.8 13.3 %all_gather.6 = bf16[64,1024]{1,0:T(8,128)(2,1)S(1)} all-gather(bf16[16,1024]{1,0:T(8,128)(2,1)S(1)} %multiply_convert_fusion.1), channel_id=1, replica_groups=mesh['req'=4,'seq'=32] {'req'}, dimensions={0}, use_global_device_ids=true | all-gather | bytes 163840 | tf_op jit(solution)/shard_map/all_gather | solution.py:93
  24.2 2.4 fusion.7
  26.5 4.3 %all-to-all-start = ((bf16[4,16,768]{2,1,0:T(8,128)(2,1)}), bf16[4,16,768]{2,1,0:T(8,128)(2,1)S(1)}, u32[]{:S(2)}, u32[]{:S(2)}) async-start(bf16[4,16,768]{2,1,0:T(8,128)(2,1)} %bitcast), calls=%async_computation | async-start | bytes 196608 | tf_op jit(solution)/shard_map/all_to_all | solution.py:97
  30.9 1.5 copy.151
  32.4 2.3 copy.153
  34.7 6.2 %copy.147 = bf16[2,1024,1024]{1,2,0:T(8,128)(2,1)} copy(bf16[2,1024,1024]{2,1,0:T(8,128)(2,1)} %param.18) | data formatting | bytes 8388608 | tf_op args[2]
  40.9 6.2 %copy.149 = bf16[2,1024,1024]{1,2,0:T(8,128)(2,1)} copy(bf16[2,1024,1024]{2,1,0:T(8,128)(2,1)} %param.19) | data formatting | bytes 8388608 | tf_op args[3]
  47.3 0.8 fusion.120
  48.1 0.1 fusion.121
  48.3 0.1 reshape_reshape_squeeze.6
  48.4 0.7 reshape_squeeze.2
  49.2 1.0 fusion.68
  50.2 0.2 copy.158
  50.4 0.1 fusion.79
  50.5 0.1 fusion.80
  50.7 0.8 copy.150
  51.6 0.8 copy.146
  52.5 0.7 reshape_reshape_squeeze.7
  53.3 0.8 copy.162
  54.1 0.3 fusion.123
  54.5 125.1 %pmax.7 = f32[2,16,4]{2,1,0:T(8,128)S(1)} all-reduce(f32[2,16,4]{2,1,0:T(8,128)S(1)} %get-tuple-element.28), channel_id=1, replica_groups=mesh['req'=4,'seq'=32] {'seq'}, use_global_device_ids=true, to_apply=%region_4.5 | all-reduce | flops 128 | bytes 1024 | tf_op jit(solution)/shard_map/pmax | solution.py:41
  179.5 0.2 fusion.64
  179.7 3.1 fusion.124
  182.8 0.4 fusion.15
  183.2 1.2 fusion.17
  184.5 0.4 convolution_multiply_fusion.3
  184.9 123.9 %all-reduce = (f32[2,16,4,64]{3,2,1,0:T(4,128)S(1)}, f32[2,16,4]{2,1,0:T(8,128)S(1)}) all-reduce(f32[2,16,4,64]{3,2,1,0:T(4,128)S(1)} %convolution_multiply_fusion.3, f32[2,16,4]{2,1,0:T(8,128)S(1)} %get-tuple-element.13), channel_id=1, replica_groups=mesh['req'=4,'seq'=32] {'seq'}, use_global_device_ids=true, to_apply=%region_5.6 | all-reduce | flops 8320 | bytes 66560 | tf_op jit(solution)/shard_map/psum | solution.py:43
  308.8 0.3 fusion.14
  309.1 0.1 convert_element_type.54
  309.3 9.8 %all_to_all.32 = bf16[16,4,256]{2,0,1:T(8,128)(2,1)S(1)} all-to-all(bf16[16,4,256]{2,0,1:T(8,128)(2,1)S(1)} %copy.166), channel_id=1, replica_groups=mesh['req'=4,'seq'=32] {'req'}, dimensions={1} | all-to-all | bytes 65536 | tf_op jit(solution)/shard_map/all_to_all | solution.py:115
  319.0 0.9 fusion.127
  320.0 15.6 %reduce-scatter.3.cloned.1.call-done = f32[16,1024]{1,0:T(8,128)} async-done(((f32[64,1024]{1,0:T(8,128)}), f32[16,1024]{1,0:T(8,128)}) %reduce-scatter.3.cloned.1.call-update) | async-done | bytes 65552 | tf_op jit(solution)/shard_map/reduce_scatter | solution.py:116
  335.6 1.0 fusion.116
  336.6 0.2 multiply_reduce_fusion
  336.9 12.0 %all_gather.7 = bf16[64,1024]{1,0:T(8,128)(2,1)S(1)} all-gather(bf16[16,1024]{1,0:T(8,128)(2,1)S(1)} %multiply_convert_fusion), channel_id=1, replica_groups=mesh['req'=4,'seq'=32] {'req'}, dimensions={0}, use_global_device_ids=true | all-gather | bytes 163840 | tf_op jit(solution)/shard_map/all_gather | solution.py:125
  348.9 3.7 fusion.32
  352.7 0.6 slice.81
  353.3 0.6 slice.79
  354.0 0.6 slice.77
  354.6 0.6 slice.75
  355.2 18.3 %reduce-scatter.5.cloned.1.call-done = f32[16,1024]{1,0:T(8,128)} async-done(((f32[64,1024]{1,0:T(8,128)}), f32[16,1024]{1,0:T(8,128)}) %reduce-scatter.5.cloned.1.call-update) | async-done | bytes 65552 | tf_op jit(solution)/shard_map/reduce_scatter | solution.py:131
  373.6 0.8 add_convert_fusion
  374.4 0.6 slice.73
  375.0 0.6 slice.71
  (60 shorter events, 1.3 us)
Async XLA Ops:
  7.2 341.7 %copy-start = (bf16[1024,1024]{1,0:T(8,128)(2,1)S(1)}, bf16[1024,1024]{1,0:T(8,128)(2,1)}, u32[]{:S(2)}) copy-start(bf16[1024,1024]{1,0:T(8,128)(2,1)} %param.31) | copy-start | bytes 6291460
  7.2 23.6 %copy-start.11 = (s32[2]{0:T(128)S(1)}, s32[2]{0:T(128)}, u32[]{:S(2)}) copy-start(s32[2]{0:T(128)} %param.22) | copy-start | bytes 28
  26.5 20.7 %all-to-all-start = ((bf16[4,16,768]{2,1,0:T(8,128)(2,1)}), bf16[4,16,768]{2,1,0:T(8,128)(2,1)S(1)}, u32[]{:S(2)}, u32[]{:S(2)}) async-start(bf16[4,16,768]{2,1,0:T(8,128)(2,1)} %bitcast), calls=%async_computation | async-start | bytes 196608 | tf_op jit(solution)/shard_map/all_to_all | solution.py:97
  30.8 304.9 %reduce-scatter.3.cloned.1.call-start = ((), (), s32[]{:S(2)}) async-start(), calls=%async_computation.4 | async-start | bytes 327680 | tf_op jit(solution)/shard_map/reduce_scatter | solution.py:116
  40.9 6.2 %copy-start.12 = (s32[2]{0:T(128)S(1)}, s32[2]{0:T(128)}, u32[]{:S(2)}) copy-start(s32[2]{0:T(128)} %param.23) | copy-start | bytes 28
  179.5 3.7 copy-start.1
  182.8 1.7 copy-start.2
  183.2 125.6 %copy-start.8 = (bf16[4,16,4,4]{3,2,1,0:T(4,128)(2,1)S(1)}, bf16[4,16,4,4]{3,2,1,0:T(4,128)(2,1)}, u32[]{:S(2)}) copy-start(bf16[4,16,4,4]{3,2,1,0:T(4,128)(2,1)} %copy.162) | copy-start | bytes 6148
  183.2 125.6 %copy-start.9 = (bf16[4,4,16,64]{3,2,1,0:T(8,128)(2,1)S(1)}, bf16[4,4,16,64]{3,2,1,0:T(8,128)(2,1)}, u32[]{:S(2)}) copy-start(bf16[4,4,16,64]{3,2,1,0:T(8,128)(2,1)} %reshape_reshape_squeeze.7) | copy-start | bytes 98308
  184.4 134.6 %copy-start.3 = (bf16[256,1024]{1,0:T(8,128)(2,1)S(1)}, bf16[256,1024]{1,0:T(8,128)(2,1)}, u32[]{:S(2)}) copy-start(bf16[256,1024]{1,0:T(8,128)(2,1)} %param.29) | copy-start | bytes 1572868
  184.4 152.4 %copy-start.10 = (f32[1024]{0:T(1024)S(1)}, f32[1024]{0:T(1024)}, u32[]{:S(2)}) copy-start(f32[1024]{0:T(1024)} %param.25) | copy-start | bytes 12292
  320.0 53.6 %reduce-scatter.5.cloned.1.call-start = ((), (), s32[]{:S(2)}) async-start(), calls=%async_computation.5 | async-start | bytes 327680 | tf_op jit(solution)/shard_map/reduce_scatter | solution.py:131
  348.9 3.8 copy-start.7
  348.9 4.4 %copy-start.6 = (bf16[8,4,1,256]{3,2,0,1:T(2,128)(2,1)S(1)}, bf16[8,4,1,256]{3,2,0,1:T(2,128)(2,1)}, u32[]{:S(2)}) copy-start(bf16[8,4,1,256]{3,2,0,1:T(2,128)(2,1)} %get-tuple-element.16) | copy-start | bytes 49156
  348.9 5.0 %copy-start.5 = (bf16[8,4,1,256]{3,2,0,1:T(2,128)(2,1)S(1)}, bf16[8,4,1,256]{3,2,0,1:T(2,128)(2,1)}, u32[]{:S(2)}) copy-start(bf16[8,4,1,256]{3,2,0,1:T(2,128)(2,1)} %get-tuple-element.17) | copy-start | bytes 49156
  348.9 5.7 %copy-start.4 = (bf16[8,4,1,256]{3,2,0,1:T(2,128)(2,1)S(1)}, bf16[8,4,1,256]{3,2,0,1:T(2,128)(2,1)}, u32[]{:S(2)}) copy-start(bf16[8,4,1,256]{3,2,0,1:T(2,128)(2,1)} %get-tuple-element.18) | copy-start | bytes 49156
Sparse Core Ops, SparseCore 0:
  320.1 15.5 reduce-scatter.2
  352.8 20.7 reduce-scatter.4
where the time goes:
time: 384 us; the launch traced here: 382 us
  blocking collectives  284 us (74%)
  waiting for transfers between devices  34 us (9%)
  local copies, waits for them, and re-layouts  26 us (7%)
  between operations  14.3 us (4%)
  matrix products  13.4 us (3%)
  other arithmetic  6.54 us (2%)
  starting transfers between devices  4.3 us (1%)
    pmax x1, blocking collectives, merge_long(): top = lax.pmax(peak, 'seq')  125 us
    psum x1, blocking collectives, merge_long(): lax.psum((total * scale, output * scale[..., None]), 'seq')  124 us
    reduce_scatter x1, waiting for transfers between devices, shards(): lax.psum_scatter(jnp.dot(hidden, w_down, preferred_element_type=jnp.float...  18.3 us
    unnamed x32, local copies, waits for them, and re-layouts  16.5 us
    reduce_scatter x1, waiting for transfers between devices, shards(): lax.psum_scatter(jnp.dot(spread, w_out, preferred_element_type=jnp.float3...  15.6 us
    all_gather x1, blocking collectives, shards(): lax.all_gather(normed, 'req', axis=0, tiled=True)  13.3 us
    all_gather x1, blocking collectives, shards(): lax.all_gather(normed_ffn, 'req', axis=0, tiled=True)  12 us
    all_to_all x1, blocking collectives, shards(): lax.all_to_all(attended, 'req', split_axis=1, concat_axis=0, tiled=True)  9.76 us
  transfers between devices with their start and end apart: 3, of which 2 were waited for; matrix products, arithmetic and copies ran while one was open for 5% of the time, Pallas kernels for 0%

commit v1 on v0

--- a/solution.py
+++ b/solution.py
@@ -112,7 +112,12 @@
     peak, total, output = join(cache_part, fresh)
     attended = output / total[..., None]
     attended = attended.transpose(0, 2, 1, 3).reshape(rows_count, width).astype(jnp.bfloat16)
-    spread = lax.all_to_all(attended, "req", split_axis=1, concat_axis=0, tiled=True)
+    spread = jnp.concatenate(
+        jax.lax.all_to_all(
+            jnp.stack(jnp.split(attended, jax.lax.axis_size("req"), axis=1), axis=0), "req", 0, 0
+        ),
+        axis=0,
+    )
     mixed = rows + lax.psum_scatter(
         jnp.dot(spread, w_out, preferred_element_type=jnp.float32),
         "req",

time: 384 us -> 384 us (level)
  no operation moved by 1% of the time
where the time goes in v1:
time: 384 us; the launch traced here: 382 us
  blocking collectives  284 us (74%)
  waiting for transfers between devices  34 us (9%)
  local copies, waits for them, and re-layouts  26 us (7%)
  between operations  14.3 us (4%)
  matrix products  13.4 us (3%)
  other arithmetic  6.55 us (2%)
  starting transfers between devices  4.3 us (1%)
    pmax x1, blocking collectives, merge_long(): top = lax.pmax(peak, 'seq')  125 us
    psum x1, blocking collectives, merge_long(): lax.psum((total * scale, output * scale[..., None]), 'seq')  124 us
    reduce_scatter x1, waiting for transfers between devices, shards(): lax.psum_scatter(jnp.dot(hidden, w_down, preferred_element_type=jnp.float...  18.3 us
    unnamed x32, local copies, waits for them, and re-layouts  16.5 us
    reduce_scatter x1, waiting for transfers between devices, shards(): lax.psum_scatter(jnp.dot(spread, w_out, preferred_element_type=jnp.float3...  15.6 us
    all_gather x1, blocking collectives, shards(): lax.all_gather(normed, 'req', axis=0, tiled=True)  13.3 us
    all_gather x1, blocking collectives, shards(): lax.all_gather(normed_ffn, 'req', axis=0, tiled=True)  12 us
    all_to_all x1, blocking collectives, shards(): jax.lax.all_to_all(jnp.stack(jnp.split(attended, jax.lax.axis_size('req')...  9.76 us
  transfers between devices with their start and end apart: 3, of which 2 were waited for; matrix products, arithmetic and copies ran while one was open for 5% of the time, Pallas kernels for 0%

profile of v1, /device:TPU:0, one launch (start us, length us, event | category | flops | bytes accessed | tf_op | source)
XLA Modules:
  0.0 382.5 jit_solution(9804030382740199844)
XLA Ops:
  7.2 1.0 fusion.115
  8.3 0.9 multiply_reduce_fusion.1
  9.2 0.8 maximum_convert_fusion
  10.1 0.8 multiply_convert_fusion.1
  10.8 13.3 %all_gather.6 = bf16[64,1024]{1,0:T(8,128)(2,1)S(1)} all-gather(bf16[16,1024]{1,0:T(8,128)(2,1)S(1)} %multiply_convert_fusion.1), channel_id=1, replica_groups=mesh['req'=4,'seq'=32] {'req'}, dimensions={0}, use_global_device_ids=true | all-gather | bytes 163840 | tf_op jit(solution)/shard_map/all_gather | solution.py:93
  24.2 2.4 fusion.7
  26.5 4.3 %all-to-all-start = ((bf16[4,16,768]{2,1,0:T(8,128)(2,1)}), bf16[4,16,768]{2,1,0:T(8,128)(2,1)S(1)}, u32[]{:S(2)}, u32[]{:S(2)}) async-start(bf16[4,16,768]{2,1,0:T(8,128)(2,1)} %bitcast), calls=%async_computation | async-start | bytes 196608 | tf_op jit(solution)/shard_map/all_to_all | solution.py:97
  30.9 1.5 copy.146
  32.4 2.3 copy.148
  34.7 6.2 %copy.142 = bf16[2,1024,1024]{1,2,0:T(8,128)(2,1)} copy(bf16[2,1024,1024]{2,1,0:T(8,128)(2,1)} %param.18) | data formatting | bytes 8388608 | tf_op args[2]
  40.9 6.2 %copy.144 = bf16[2,1024,1024]{1,2,0:T(8,128)(2,1)} copy(bf16[2,1024,1024]{2,1,0:T(8,128)(2,1)} %param.19) | data formatting | bytes 8388608 | tf_op args[3]
  47.3 0.8 fusion.120
  48.1 0.1 fusion.121
  48.3 0.1 reshape_reshape_squeeze.6
  48.4 0.7 reshape_squeeze.2
  49.2 1.0 fusion.68
  50.2 0.2 copy.153
  50.4 0.1 fusion.79
  50.5 0.1 fusion.80
  50.7 0.8 copy.145
  51.6 0.8 copy.141
  52.5 0.7 reshape_reshape_squeeze.7
  53.3 0.8 copy.157
  54.1 0.3 fusion.123
  54.5 125.1 %pmax.7 = f32[2,16,4]{2,1,0:T(8,128)S(1)} all-reduce(f32[2,16,4]{2,1,0:T(8,128)S(1)} %get-tuple-element.32), channel_id=1, replica_groups=mesh['req'=4,'seq'=32] {'seq'}, use_global_device_ids=true, to_apply=%region_4.5 | all-reduce | flops 128 | bytes 1024 | tf_op jit(solution)/shard_map/pmax | solution.py:41
  179.5 0.2 fusion.64
  179.7 3.1 fusion.124
  182.8 0.4 fusion.15
  183.2 1.2 fusion.17
  184.5 0.4 convolution_multiply_fusion.3
  184.9 123.9 %all-reduce = (f32[2,16,4,64]{3,2,1,0:T(4,128)S(1)}, f32[2,16,4]{2,1,0:T(8,128)S(1)}) all-reduce(f32[2,16,4,64]{3,2,1,0:T(4,128)S(1)} %convolution_multiply_fusion.3, f32[2,16,4]{2,1,0:T(8,128)S(1)} %get-tuple-element.13), channel_id=1, replica_groups=mesh['req'=4,'seq'=32] {'seq'}, use_global_device_ids=true, to_apply=%region_5.6 | all-reduce | flops 8320 | bytes 66560 | tf_op jit(solution)/shard_map/psum | solution.py:43
  308.8 0.3 fusion.14
  309.1 0.1 convert_element_type.53
  309.3 9.8 %all_to_all.21 = bf16[4,16,256]{2,1,0:T(8,128)(2,1)S(1)} all-to-all(bf16[4,16,256]{2,1,0:T(8,128)(2,1)S(1)} %pad_maximum_fusion.1), channel_id=1, replica_groups=mesh['req'=4,'seq'=32] {'req'}, dimensions={0} | all-to-all | bytes 65536 | tf_op jit(solution)/shard_map/all_to_all | solution.py:116
  319.0 0.9 fusion.127
  320.0 15.6 %reduce-scatter.3.cloned.1.call-done = f32[16,1024]{1,0:T(8,128)} async-done(((f32[64,1024]{1,0:T(8,128)}), f32[16,1024]{1,0:T(8,128)}) %reduce-scatter.3.cloned.1.call-update) | async-done | bytes 65552 | tf_op jit(solution)/shard_map/reduce_scatter | solution.py:121
  335.7 1.0 fusion.116
  336.6 0.2 multiply_reduce_fusion
  336.9 12.0 %all_gather.7 = bf16[64,1024]{1,0:T(8,128)(2,1)S(1)} all-gather(bf16[16,1024]{1,0:T(8,128)(2,1)S(1)} %multiply_convert_fusion), channel_id=1, replica_groups=mesh['req'=4,'seq'=32] {'req'}, dimensions={0}, use_global_device_ids=true | all-gather | bytes 163840 | tf_op jit(solution)/shard_map/all_gather | solution.py:130
  348.9 3.7 fusion.32
  352.7 0.6 slice.81
  353.3 0.6 slice.79
  354.0 0.6 slice.77
  354.6 0.6 slice.75
  355.2 18.3 %reduce-scatter.5.cloned.1.call-done = f32[16,1024]{1,0:T(8,128)} async-done(((f32[64,1024]{1,0:T(8,128)}), f32[16,1024]{1,0:T(8,128)}) %reduce-scatter.5.cloned.1.call-update) | async-done | bytes 65552 | tf_op jit(solution)/shard_map/reduce_scatter | solution.py:136
  373.6 0.8 add_convert_fusion
  374.4 0.6 slice.73
  375.0 0.6 slice.71
  (61 shorter events, 1.3 us)
Async XLA Ops:
  7.2 341.7 %copy-start = (bf16[1024,1024]{1,0:T(8,128)(2,1)S(1)}, bf16[1024,1024]{1,0:T(8,128)(2,1)}, u32[]{:S(2)}) copy-start(bf16[1024,1024]{1,0:T(8,128)(2,1)} %param.31) | copy-start | bytes 6291460
  7.2 23.6 %copy-start.11 = (s32[2]{0:T(128)S(1)}, s32[2]{0:T(128)}, u32[]{:S(2)}) copy-start(s32[2]{0:T(128)} %param.22) | copy-start | bytes 28
  26.5 20.7 %all-to-all-start = ((bf16[4,16,768]{2,1,0:T(8,128)(2,1)}), bf16[4,16,768]{2,1,0:T(8,128)(2,1)S(1)}, u32[]{:S(2)}, u32[]{:S(2)}) async-start(bf16[4,16,768]{2,1,0:T(8,128)(2,1)} %bitcast), calls=%async_computation | async-start | bytes 196608 | tf_op jit(solution)/shard_map/all_to_all | solution.py:97
  30.8 304.9 %reduce-scatter.3.cloned.1.call-start = ((), (), s32[]{:S(2)}) async-start(), calls=%async_computation.4 | async-start | bytes 327680 | tf_op jit(solution)/shard_map/reduce_scatter | solution.py:121
  40.9 6.2 %copy-start.12 = (s32[2]{0:T(128)S(1)}, s32[2]{0:T(128)}, u32[]{:S(2)}) copy-start(s32[2]{0:T(128)} %param.23) | copy-start | bytes 28
  179.5 3.7 copy-start.1
  182.8 1.7 copy-start.2
  183.2 125.6 %copy-start.8 = (bf16[4,16,4,4]{3,2,1,0:T(4,128)(2,1)S(1)}, bf16[4,16,4,4]{3,2,1,0:T(4,128)(2,1)}, u32[]{:S(2)}) copy-start(bf16[4,16,4,4]{3,2,1,0:T(4,128)(2,1)} %copy.157) | copy-start | bytes 6148
  183.2 125.6 %copy-start.9 = (bf16[4,4,16,64]{3,2,1,0:T(8,128)(2,1)S(1)}, bf16[4,4,16,64]{3,2,1,0:T(8,128)(2,1)}, u32[]{:S(2)}) copy-start(bf16[4,4,16,64]{3,2,1,0:T(8,128)(2,1)} %reshape_reshape_squeeze.7) | copy-start | bytes 98308
  184.4 134.6 %copy-start.3 = (bf16[256,1024]{1,0:T(8,128)(2,1)S(1)}, bf16[256,1024]{1,0:T(8,128)(2,1)}, u32[]{:S(2)}) copy-start(bf16[256,1024]{1,0:T(8,128)(2,1)} %param.29) | copy-start | bytes 1572868
  184.4 152.4 %copy-start.10 = (f32[1024]{0:T(1024)S(1)}, f32[1024]{0:T(1024)}, u32[]{:S(2)}) copy-start(f32[1024]{0:T(1024)} %param.25) | copy-start | bytes 12292
  320.0 53.6 %reduce-scatter.5.cloned.1.call-start = ((), (), s32[]{:S(2)}) async-start(), calls=%async_computation.5 | async-start | bytes 327680 | tf_op jit(solution)/shard_map/reduce_scatter | solution.py:136
  348.9 3.8 copy-start.7
  348.9 4.4 %copy-start.6 = (bf16[8,4,1,256]{3,2,0,1:T(2,128)(2,1)S(1)}, bf16[8,4,1,256]{3,2,0,1:T(2,128)(2,1)}, u32[]{:S(2)}) copy-start(bf16[8,4,1,256]{3,2,0,1:T(2,128)(2,1)} %get-tuple-element.16) | copy-start | bytes 49156
  348.9 5.0 %copy-start.5 = (bf16[8,4,1,256]{3,2,0,1:T(2,128)(2,1)S(1)}, bf16[8,4,1,256]{3,2,0,1:T(2,128)(2,1)}, u32[]{:S(2)}) copy-start(bf16[8,4,1,256]{3,2,0,1:T(2,128)(2,1)} %get-tuple-element.17) | copy-start | bytes 49156
  348.9 5.7 %copy-start.4 = (bf16[8,4,1,256]{3,2,0,1:T(2,128)(2,1)S(1)}, bf16[8,4,1,256]{3,2,0,1:T(2,128)(2,1)}, u32[]{:S(2)}) copy-start(bf16[8,4,1,256]{3,2,0,1:T(2,128)(2,1)} %get-tuple-element.18) | copy-start | bytes 49156
Sparse Core Ops, SparseCore 0:
  320.1 15.5 reduce-scatter.2
  352.8 20.7 reduce-scatter.4
